TPU v7x, 256 devices: a whole 4x4x8 slice. The times are simulated.
256 devices in a mesh: tok: 64 (over y, z, core), head: 4 (over x).
Axes of the slice: x: 4, y: 4, z: 8, core: 2. Of those that a mesh axis runs over, the one named last changes fastest.
Arguments:
- hidden: bfloat16 [2048, 2048], P('tok', 'head'), may hold values from -24 to 24
- attn_gain: float32 [2048], replicated, may hold values from 0.1 to 1.9
- w_query: bfloat16 [2048, 3072], P(None, 'head'), may hold values from -0.125 to 0.125
- w_latent: bfloat16 [2048, 576], P('head'), may hold values from -0.125 to 0.125
- w_key_up: bfloat16 [16, 128, 512], P('head'), may hold values from -0.5 to 0.5
- w_value_up: bfloat16 [16, 512, 128], P('head'), may hold values from -1 to 1
- w_out: bfloat16 [2048, 2048], P('head'), may hold values from -0.125 to 0.125
- latent_cache: bfloat16 [638976, 576], P(('tok', 'head')), may hold values from -6 to 6
- cache_lengths: int32 [2048], P('tok'), may hold values from 144 to 2048, as said below
- request_slot: int32 [2048], P('tok'), may hold values from 0 to 2047, as said below
- ffn_gain: float32 [2048], P('head'), may hold values from 0.1 to 1.9
- w_router: bfloat16 [2048, 64], P('head'), may hold values from -0.25 to 0.25
- routes: int32 [2048, 6], P('tok'), may hold values from 0 to 63, all different within a row; in each aligned block of 32 rows (0 to 31, 32 to 63, ...) at most 6 rows name the same one
- expert_gate: bfloat16 [64, 2048, 1408], P('tok', None, 'head'), may hold values from -0.125 to 0.125
- expert_up: bfloat16 [64, 2048, 1408], P('tok', None, 'head'), may hold values from -0.125 to 0.125
- expert_down: bfloat16 [64, 1408, 2048], P('tok', 'head'), may hold values from -0.15625 to 0.15625
Outputs:
- new_entry: bfloat16 [2048, 576], P('tok')
- attended: bfloat16 [2048, 2048], P('tok', 'head')
- expert_mix: bfloat16 [2048, 2048], P('tok', 'head')
Inputs may be any that keep to these rules, and one draw needn't show every extreme that they name: `request_slot`: a permutation of the 2048 slots; slot s lies on owner s // 32, so every owner holds 32 slots; the requests of one device name at most 1 slots of one owner, and every device reaches that bound. `cache_lengths`: the caches of an owner's slots lie end to end in slot order at the start of that owner's 9984 rows of latent_cache; they fill at most 9984 rows, and some owner fills all of them. `routes`: each row names 6 different experts; in the rows of one device no expert is named more than 6 times.
All inputs are finite; a program needn't handle non-finite values.
Results may differ from a plain program's by a relative error of at most 0.028.
Values may be sent and summed in bfloat16 or wider, within the bound.
No kernel may reach another device: no remote copies, remote signals or barrier semaphores. Data moves between devices by JAX's collectives and lax.ppermute only.
A program may use at most 128 MiB of HBM per device.

v0:
```python
import jax
import jax.numpy as jnp
from jax import lax
from jax.sharding import PartitionSpec as P

D = 2048
NOPE = 128
ROPE = 64
LATENT = 512
NORM_EPS = 1e-06


def rotate_pairs(values, places):
    halfway = values.shape[-1] // 2
    freqs = 10000.0 ** (-jnp.arange(halfway, dtype=jnp.float32) / halfway)
    angles = places.astype(jnp.float32).reshape(places.shape + (1,) * (values.ndim - 1)) * freqs
    cosine = jnp.cos(angles)
    sine = jnp.sin(angles)
    first_half = values[..., :halfway]
    second_half = values[..., halfway:]
    return jnp.concatenate(
        [first_half * cosine - second_half * sine, first_half * sine + second_half * cosine],
        axis=-1,
    )


def owner_attend(all_heads, owner_lengths, latent_cache, head_index, factor):
    slot_rows = all_heads.shape[0]
    total_heads = all_heads.shape[1]
    probe_width = all_heads.shape[2]
    key_rows = latent_cache.shape[0]
    starts = jnp.cumsum(owner_lengths) - owner_lengths
    places = head_index * key_rows + jnp.arange(key_rows, dtype=jnp.int32)
    inside = (places[None, :] >= starts[:, None]) & (
        places[None, :] < (starts + owner_lengths)[:, None]
    )
    scores = factor * jnp.einsum(
        "qc,pc->qp",
        all_heads.reshape(slot_rows * total_heads, probe_width),
        latent_cache,
        preferred_element_type=jnp.float32,
    )
    scores = scores.reshape(slot_rows, total_heads, key_rows)
    weights = jnp.where(inside[:, None, :], jnp.exp(scores), 0.0).astype(jnp.bfloat16)
    numerator = jnp.einsum(
        "khp,pl->khl", weights, latent_cache[:, :LATENT], preferred_element_type=jnp.float32
    )
    denominator = jnp.sum(weights.astype(jnp.float32), axis=2)
    return (numerator, denominator)


def body(
    hidden,
    attn_gain,
    w_query,
    w_latent,
    w_key_up,
    w_value_up,
    w_out,
    latent_cache,
    cache_lengths,
    request_slot,
    ffn_gain,
    w_router,
    routes,
    expert_gate,
    expert_up,
    expert_down,
):
    local_rows = hidden.shape[0]
    quarter_width = hidden.shape[1]
    local_heads = w_key_up.shape[0]
    peer_count = lax.axis_size("tok")
    head_index = lax.axis_index("head")
    tok_index = lax.axis_index("tok")
    row_ids = jnp.arange(local_rows, dtype=jnp.int32)
    gathered = lax.all_gather(hidden, "head", axis=1, tiled=True)
    widened = gathered.astype(jnp.float32)
    inv_attn = lax.rsqrt(jnp.mean(widened * widened, axis=1, keepdims=True) + NORM_EPS)
    normed_attn = (widened * inv_attn * attn_gain).astype(jnp.bfloat16)
    normed_part = lax.dynamic_slice_in_dim(
        normed_attn, head_index * quarter_width, quarter_width, 1
    )
    compressed = lax.psum(
        jnp.dot(normed_part, w_latent, preferred_element_type=jnp.float32), "head"
    )
    latent_new = compressed[:, :LATENT]
    latent_new = latent_new * lax.rsqrt(
        jnp.mean(latent_new * latent_new, axis=1, keepdims=True) + NORM_EPS
    )
    new_entry = jnp.concatenate(
        [latent_new, rotate_pairs(compressed[:, LATENT:], cache_lengths)], axis=1
    ).astype(jnp.bfloat16)
    queries = jnp.dot(normed_attn, w_query, preferred_element_type=jnp.float32).astype(jnp.bfloat16)
    queries = queries.reshape(local_rows, local_heads, NOPE + ROPE)
    absorbed = jnp.einsum(
        "bhn,hnl->bhl", queries[:, :, :NOPE], w_key_up, preferred_element_type=jnp.float32
    ).astype(jnp.bfloat16)
    turned = rotate_pairs(queries[:, :, NOPE:].astype(jnp.float32), cache_lengths).astype(
        jnp.bfloat16
    )
    probes = jnp.concatenate([absorbed, turned], axis=2)
    factor = (NOPE + ROPE) ** (-0.5)
    owner_ids = jnp.arange(peer_count, dtype=jnp.int32)
    dest_owner = request_slot // local_rows
    goes_to = dest_owner[None, :] == owner_ids[:, None]
    sent_any = jnp.max(goes_to.astype(jnp.int32), axis=1)
    sent_row = jnp.sum(jnp.where(goes_to, row_ids[None, :], 0), axis=1) + local_rows * (
        1 - sent_any
    )
    packed = jnp.concatenate([probes, new_entry[:, None, :]], axis=1)
    packed = jnp.concatenate([packed, jnp.zeros((1,) + packed.shape[1:], jnp.bfloat16)], axis=0)
    send_ints = jnp.stack(
        [
            jnp.where(sent_any > 0, request_slot[jnp.minimum(sent_row, local_rows - 1)], -1),
            cache_lengths[jnp.minimum(sent_row, local_rows - 1)],
        ],
        axis=1,
    )
    got_packed = lax.all_to_all(packed[sent_row], "tok", 0, 0, tiled=True)
    got_ints = lax.all_to_all(send_ints, "tok", 0, 0, tiled=True)
    got_slot = got_ints[:, 0]
    local_slot = got_slot - tok_index * local_rows
    slot_sel = local_slot[None, :] == row_ids[:, None]
    src_of_slot = jnp.sum(jnp.where(slot_sel, owner_ids[None, :], 0), axis=1)
    owner_packed = got_packed[src_of_slot]
    owner_probes = owner_packed[:, :local_heads]
    owner_new = owner_packed[:, local_heads]
    owner_lengths = got_ints[src_of_slot, 1]
    all_heads = lax.all_gather(owner_probes, "head", axis=1, tiled=True)
    numerator, denominator = owner_attend(
        all_heads, owner_lengths, latent_cache, head_index, factor
    )
    joined = lax.psum_scatter(
        jnp.concatenate([numerator, denominator[:, :, None]], axis=2),
        "head",
        scatter_dimension=1,
        tiled=True,
    )
    group_num = joined[:, :, :LATENT]
    group_den = joined[:, :, LATENT]
    self_score = factor * jnp.einsum(
        "bhc,bc->bh", owner_probes, owner_new, preferred_element_type=jnp.float32
    )
    self_weight = jnp.exp(self_score).astype(jnp.bfloat16).astype(jnp.float32)
    total_num = group_num + self_weight[:, :, None] * owner_new[:, None, :LATENT].astype(
        jnp.float32
    )
    total_den = group_den + self_weight
    mixed_latent = (total_num / total_den[:, :, None]).astype(jnp.bfloat16)
    owner_out = jnp.einsum(
        "bhl,hld->bhd", mixed_latent, w_value_up, preferred_element_type=jnp.float32
    ).astype(jnp.bfloat16)
    owner_out = owner_out.reshape(local_rows, local_heads * NOPE)
    owner_out = jnp.concatenate(
        [owner_out, jnp.zeros((1, local_heads * NOPE), jnp.bfloat16)], axis=0
    )
    back_valid = (local_slot >= 0) & (local_slot < local_rows)
    back_row = jnp.where(back_valid, local_slot, local_rows)
    returned_out = lax.all_to_all(owner_out[back_row], "tok", 0, 0, tiled=True)
    head_out = returned_out[dest_owner]
    head_out = head_out.reshape(local_rows, local_heads * NOPE)
    attn_piece = lax.psum_scatter(
        jnp.dot(head_out, w_out, preferred_element_type=jnp.float32),
        "head",
        scatter_dimension=1,
        tiled=True,
    )
    attended = (hidden.astype(jnp.float32) + attn_piece).astype(jnp.bfloat16)
    attended_wide = attended.astype(jnp.float32)
    gained = (attended_wide * ffn_gain).astype(jnp.bfloat16)
    squares, logit_part = lax.psum(
        (
            jnp.sum(attended_wide * attended_wide, axis=1),
            jnp.dot(gained, w_router, preferred_element_type=jnp.float32),
        ),
        "head",
    )
    inv_ffn = lax.rsqrt(squares / D + NORM_EPS)
    logits = logit_part * inv_ffn[:, None]
    normed_ffn = (attended_wide * ffn_gain * inv_ffn[:, None]).astype(jnp.bfloat16)
    expert_count = w_router.shape[1]
    route_count = routes.shape[1]
    expert_ids = jnp.arange(expert_count, dtype=jnp.int32)
    named = routes[:, :, None] == expert_ids[None, None, :]
    picked = jnp.sum(jnp.where(named, logits[:, None, :], 0.0), axis=2)
    lifted = jnp.exp(picked)
    route_weight = lifted / jnp.sum(lifted, axis=1, keepdims=True)
    struck = jnp.max(named.astype(jnp.int32), axis=1)
    earlier_hits = jnp.cumsum(struck, axis=0) - struck
    capacity = min(local_rows, max(2, 2 * local_rows * route_count // expert_count))
    route_place = routes * capacity + jnp.take_along_axis(earlier_hits, routes, axis=1)
    slot_total = expert_count * capacity
    slot_ids = jnp.arange(slot_total, dtype=jnp.int32)
    filled = route_place[None, :, :] == slot_ids[:, None, None]
    source_token = jnp.sum(
        jnp.where(filled, row_ids[None, :, None], 0), axis=(1, 2)
    ) + local_rows * (1 - jnp.max(filled.astype(jnp.int32), axis=(1, 2)))
    full_rows = lax.all_gather(normed_ffn, "head", axis=1, tiled=True)
    padded_rows = jnp.concatenate(
        [full_rows, jnp.zeros((1, full_rows.shape[1]), jnp.bfloat16)], axis=0
    )
    arrived = lax.all_to_all(
        padded_rows[source_token].reshape(expert_count, capacity, full_rows.shape[1]),
        "tok",
        split_axis=0,
        concat_axis=0,
        tiled=True,
    )
    expert_in = arrived.reshape(peer_count * capacity, full_rows.shape[1])
    gate_value = jnp.dot(expert_in, expert_gate[0], preferred_element_type=jnp.float32)
    up_value = jnp.dot(expert_in, expert_up[0], preferred_element_type=jnp.float32)
    activity = (jax.nn.silu(gate_value) * up_value).astype(jnp.bfloat16)
    expert_share = lax.psum_scatter(
        jnp.dot(activity, expert_down[0], preferred_element_type=jnp.float32).astype(jnp.bfloat16),
        "head",
        scatter_dimension=1,
        tiled=True,
    )
    returned = lax.all_to_all(
        expert_share.reshape(peer_count, capacity, quarter_width),
        "tok",
        split_axis=0,
        concat_axis=0,
        tiled=True,
    )
    chosen_rows = returned.reshape(slot_total, quarter_width)[route_place]
    expert_mix = jnp.sum(route_weight[:, :, None] * chosen_rows.astype(jnp.float32), axis=1).astype(
        jnp.bfloat16
    )
    return (new_entry, attended, expert_mix)


def solution(mesh):
    in_specs = (
        P("tok", "head"),
        P(),
        P(None, "head"),
        P("head", None),
        P("head", None, None),
        P("head", None, None),
        P("head", None),
        P(("tok", "head"), None),
        P("tok"),
        P("tok"),
        P("head"),
        P("head", None),
        P("tok", None),
        P("tok", None, "head"),
        P("tok", None, "head"),
        P("tok", "head", None),
    )
    out_specs = (P("tok", None), P("tok", "head"), P("tok", "head"))
    return jax.shard_map(body, mesh=mesh, in_specs=in_specs, out_specs=out_specs, check_vma=False)
```

profile of v0, /device:TPU:1, one launch (start us, length us, event | category | flops | bytes accessed | tf_op | source)
XLA Modules:
  0.0 402.8 jit_solution(13905377801501472798)
XLA Ops:
  7.2 1.4 compare_select_fusion.3
  8.7 1.4 gather_fusion
  10.1 1.4 gather_fusion.1
  12.3 13.1 %all-to-all-start = ((s32[64,1,2]{2,1,0:T(1,128)}), s32[64,1,2]{2,1,0:T(1,128)S(1)}, u32[]{:S(2)}, u32[]{:S(2)}) async-start(s32[64,1,2]{2,1,0:T(1,128)} %copy.107), calls=%async_computation | async-start | bytes 65536 | tf_op jit(solution)/shard_map/all_to_all | solution.py:121
  25.5 10.3 %all_gather.9 = bf16[32,2048]{1,0:T(8,128)(2,1)S(1)} all-gather(bf16[32,512]{1,0:T(8,128)(2,1)} %param.16), channel_id=1, replica_groups=mesh['tok'=64,'head'=4] {'head'}, dimensions={1}, use_global_device_ids=true | all-gather | bytes 163840 | tf_op jit(solution)/shard_map/all_gather | solution.py:77
  36.7 2.0 fusion.45
  40.2 1.2 fusion.16
  44.3 40.8 %all-reduce.7.cloned.1.call-done = f32[32,576]{1,0:T(8,128)} async-done(((f32[32,576]{1,0:T(8,128)}), f32[32,576]{1,0:T(8,128)}) %all-reduce.7.cloned.1.call-update) | async-done | bytes 73744 | tf_op jit(solution)/shard_map/psum | solution.py:84
  85.1 1.0 multiply_reduce_fusion.1
  86.0 0.9 multiply_cosine_fusion
  87.1 0.9 fusion.76
  88.3 1.5 gather_fusion.3
  89.8 13.0 %all-to-all-start.1 = ((bf16[64,5,576]{2,1,0:T(8,128)(2,1)}), bf16[64,5,576]{2,1,0:T(8,128)(2,1)}, u32[]{:S(2)}, u32[]{:S(2)}) async-start(bf16[64,5,576]{2,1,0:T(8,128)(2,1)} %gather_fusion.3), calls=%async_computation.1 | async-start | bytes 1310720 | tf_op jit(solution)/shard_map/all_to_all | solution.py:120
  104.0 2.5 copy.117
  107.1 15.7 %all-to-all-done.1 = bf16[64,5,576]{2,1,0:T(8,128)(2,1)} async-done(((bf16[64,5,576]{2,1,0:T(8,128)(2,1)}), bf16[64,5,576]{2,1,0:T(8,128)(2,1)}, u32[]{:S(2)}, u32[]{:S(2)}) %all-to-all-start.1) | async-done | bytes 368672 | tf_op jit(solution)/shard_map/all_to_all | solution.py:120
  122.8 1.8 gather_fusion.4
  125.3 11.3 %all_gather.10 = bf16[32,16,576]{2,0,1:T(8,128)(2,1)S(1)} all-gather(bf16[32,4,576]{2,0,1:T(8,128)(2,1)S(1)} %copy.113), channel_id=1, replica_groups=mesh['tok'=64,'head'=4] {'head'}, dimensions={1}, use_global_device_ids=true | all-gather | bytes 737280 | tf_op jit(solution)/shard_map/all_gather | solution.py:130
  136.9 6.9 %convert_reduce_fusion = (f32[512]{0:T(512)}, bf16[512,2496]{0,1:T(8,128)(2,1)}) fusion(pred[512,2496]{0,1:T(32,128)(4,1)S(1)} %copy-done.2, bf16[512,576]{1,0:T(8,128)(2,1)S(1)} %bitcast.106, bf16[2496,576]{0,1:T(8,128)(2,1)} %param.23), kind=kOutput, calls=%fused_computation.11 | convolution fusion | flops 1478589952 | bytes 7301120 | tf_op jit(solution)/shard_map/qc,pc->qp/dot_general | solution.py:37
  143.8 0.9 broadcast_in_dim.142
  144.7 4.4 %copy.115 = bf16[512,2496]{1,0:T(8,128)(2,1)} copy(bf16[512,2496]{0,1:T(8,128)(2,1)} %get-tuple-element.32) | data formatting | bytes 5111808 | tf_op jit(solution)/shard_map/exp | solution.py:44
  149.1 4.1 %fusion = f32[32,16,512]{2,1,0:T(8,128)S(1)} fusion(bf16[32,16,2496]{2,1,0:T(8,128)(2,1)} %bitcast.104, bf16[2496,576]{0,1:T(8,128)(2,1)} %param.23, pred[32,2496]{1,0:T(8,128)(4,1)S(1)} %compare_and_fusion), kind=kOutput, calls=%fused_computation.15 | convolution fusion | flops 1309900800 | bytes 6371328 | tf_op jit(solution)/shard_map/khp,pl->khl/dot_general | solution.py:45
  153.4 1.5 copy.119
  155.1 1.8 fusion.35
  157.8 21.0 %reduce-scatter.4.cloned.1.call-done = f32[32,4,513]{2,0,1:T(8,128)} async-done(((f32[32,16,513]{2,0,1:T(8,128)}), f32[32,4,513]{2,0,1:T(8,128)}) %reduce-scatter.4.cloned.1.call-update) | async-done | bytes 262672 | tf_op jit(solution)/shard_map/reduce_scatter | solution.py:134
  178.8 0.9 slice_reduce_fusion
  179.7 1.4 fusion.17
  183.7 12.9 %all-to-all-start.2 = ((bf16[64,2,256]{2,1,0:T(2,128)(2,1)}), bf16[64,2,256]{2,1,0:T(2,128)(2,1)S(1)}, u32[]{:S(2)}, u32[]{:S(2)}) async-start(bf16[64,2,256]{2,1,0:T(2,128)(2,1)} %reshape.501), calls=%async_computation.3 | async-start | bytes 131072 | tf_op jit(solution)/shard_map/all_to_all | solution.py:160
  197.0 1.6 gather_fusion.9
  198.7 7.7 %all-to-all-done.2 = bf16[64,2,256]{2,1,0:T(2,128)(2,1)S(1)} async-done(((bf16[64,2,256]{2,1,0:T(2,128)(2,1)}), bf16[64,2,256]{2,1,0:T(2,128)(2,1)S(1)}, u32[]{:S(2)}, u32[]{:S(2)}) %all-to-all-start.2) | async-done | bytes 65568 | tf_op jit(solution)/shard_map/all_to_all | solution.py:160
  207.2 2.8 fusion.62
  210.3 14.0 %reduce-scatter.6.cloned.1.call-done = f32[32,512]{1,0:T(8,128)} async-done(((f32[32,2048]{1,0:T(8,128)}), f32[32,512]{1,0:T(8,128)}) %reduce-scatter.6.cloned.1.call-update) | async-done | bytes 65552 | tf_op jit(solution)/shard_map/reduce_scatter | solution.py:163
  224.3 1.0 fusion.40
  225.4 11.8 %all-reduce.4 = (f32[32]{0:T(128)S(1)}, f32[32,64]{1,0:T(8,128)S(1)}) all-reduce(f32[32]{0:T(128)S(1)} %get-tuple-element.11, f32[32,64]{1,0:T(8,128)S(1)} %fusion.41), channel_id=1, replica_groups=mesh['tok'=64,'head'=4] {'head'}, use_global_device_ids=true, to_apply=%region_12.13 | all-reduce | flops 2080 | bytes 16640 | tf_op jit(solution)/shard_map/psum | solution.py:172
  237.3 9.1 %all_gather.11 = bf16[32,2048]{1,0:T(8,128)(2,1)S(1)} all-gather(bf16[32,512]{1,0:T(8,128)(2,1)S(1)} %fusion.39), channel_id=1, replica_groups=mesh['tok'=64,'head'=4] {'head'}, dimensions={1}, use_global_device_ids=true | all-gather | bytes 163840 | tf_op jit(solution)/shard_map/all_gather | solution.py:199
  246.4 3.1 gather_fusion.7
  249.5 3.7 reshape.405
  253.2 70.5 %all_to_all.39 = bf16[64,6,2048]{2,1,0:T(8,128)(2,1)} all-to-all(bf16[64,6,2048]{2,1,0:T(8,128)(2,1)} %reshape.405), channel_id=1, replica_groups=mesh['tok'=64,'head'=4] {'tok'}, dimensions={0} | all-to-all | bytes 3145728 | tf_op jit(solution)/shard_map/all_to_all | solution.py:203
  323.7 3.7 reshape.406
  327.4 3.6 fusion.8
  331.0 5.5 %convolution_convert_fusion = bf16[384,2048]{1,0:T(8,128)(2,1)} fusion(bf16[1,352,2048]{2,1,0:T(8,128)(2,1)} %param.31, bf16[384,2048]{1,0:T(8,128)(2,1)} %reshape.406, bf16[1,2048,352]{1,2,0:T(8,128)(2,1)} %param.30, f32[384,352]{0,1:T(8,128)} %fusion.8), kind=kOutput, calls=%fused_computation.14 | convolution fusion | flops 1108893696 | bytes 6569984 | tf_op jit(solution)/shard_map/dot_general | solution.py:215
  337.4 21.5 %reduce-scatter.8.cloned.1.call-done = bf16[384,512]{1,0:T(8,128)(2,1)} async-done(((bf16[384,2048]{1,0:T(8,128)(2,1)}), bf16[384,512]{1,0:T(8,128)(2,1)}) %reduce-scatter.8.cloned.1.call-update) | async-done | bytes 393232 | tf_op jit(solution)/shard_map/reduce_scatter | solution.py:214
  359.0 1.9 reshape.407
  360.9 11.7 %all-to-all-start.4 = ((bf16[64,6,512]{2,1,0:T(8,128)(2,1)}), bf16[64,6,512]{2,1,0:T(8,128)(2,1)}, u32[]{:S(2)}, u32[]{:S(2)}) async-start(bf16[64,6,512]{2,1,0:T(8,128)(2,1)} %reshape.407), calls=%async_computation.7 | async-start | bytes 1048576 | tf_op jit(solution)/shard_map/all_to_all | solution.py:220
  374.3 15.5 %all-to-all-done.4 = bf16[64,6,512]{2,1,0:T(8,128)(2,1)} async-done(((bf16[64,6,512]{2,1,0:T(8,128)(2,1)}), bf16[64,6,512]{2,1,0:T(8,128)(2,1)}, u32[]{:S(2)}, u32[]{:S(2)}) %all-to-all-start.4) | async-done | bytes 393248 | tf_op jit(solution)/shard_map/all_to_all | solution.py:220
  389.8 1.2 reshape.408
  390.9 1.7 gather_fusion.8
  392.6 1.8 reshape.488
  394.4 1.9 multiply_reduce_fusion
  (134 shorter events, 17.2 us)
Async XLA Ops:
  7.2 31.6 %copy-start = (bf16[2048,768]{1,0:T(8,128)(2,1)S(1)}, bf16[2048,768]{1,0:T(8,128)(2,1)}, u32[]{:S(2)}) copy-start(bf16[2048,768]{1,0:T(8,128)(2,1)} %param.18) | copy-start | bytes 9437188
  12.3 29.2 %all-to-all-start = ((s32[64,1,2]{2,1,0:T(1,128)}), s32[64,1,2]{2,1,0:T(1,128)S(1)}, u32[]{:S(2)}, u32[]{:S(2)}) async-start(s32[64,1,2]{2,1,0:T(1,128)} %copy.107), calls=%async_computation | async-start | bytes 65536 | tf_op jit(solution)/shard_map/all_to_all | solution.py:121
  25.5 59.6 %all-reduce.7.cloned.1.call-start = ((), (), s32[]{:S(2)}) async-start(), calls=%async_computation.8 | async-start | bytes 163840 | tf_op jit(solution)/shard_map/psum | solution.py:84
  38.7 2.7 copy-start.1
  43.7 44.4 %copy-start.18 = (s32[32]{0:T(128)}, s32[32]{0:T(128)S(1)}, u32[]{:S(2)}) copy-start(s32[32]{0:T(128)S(1)} %reduce.1) | copy-start | bytes 388
  86.0 2.1 copy-start.16
  87.0 1.0 copy-start.9
  87.0 1.0 copy-start.11
  89.8 33.0 %all-to-all-start.1 = ((bf16[64,5,576]{2,1,0:T(8,128)(2,1)}), bf16[64,5,576]{2,1,0:T(8,128)(2,1)}, u32[]{:S(2)}, u32[]{:S(2)}) async-start(bf16[64,5,576]{2,1,0:T(8,128)(2,1)} %gather_fusion.3), calls=%async_computation.1 | async-start | bytes 1310720 | tf_op jit(solution)/shard_map/all_to_all | solution.py:120
  102.7 76.0 %reduce-scatter.4.cloned.1.call-start = ((), (), s32[]{:S(2)}) async-start(), calls=%async_computation.9 | async-start | bytes 1638400 | tf_op jit(solution)/shard_map/reduce_scatter | solution.py:134
  104.0 2.5 copy-start.21
  124.6 19.2 %copy-start.3 = (bf16[32,5,576]{2,1,0:T(8,128)(2,1)}, bf16[32,5,576]{2,1,0:T(8,128)(2,1)S(1)}, u32[]{:S(2)}) copy-start(bf16[32,5,576]{2,1,0:T(8,128)(2,1)S(1)} %gather_fusion.4) | copy-start | bytes 552964
  124.6 12.3 %copy-start.2 = (pred[512,2496]{0,1:T(32,128)(4,1)S(1)}, pred[512,2496]{0,1:T(32,128)(4,1)}, u32[]{:S(2)}) copy-start(pred[512,2496]{0,1:T(32,128)(4,1)} %copy.117) | copy-start | bytes 3833860
  124.7 0.7 copy-start.5
  153.4 1.5 copy-start.14
  153.4 1.6 copy-start.19
  153.4 1.6 copy-start.4
  183.7 22.7 %all-to-all-start.2 = ((bf16[64,2,256]{2,1,0:T(2,128)(2,1)}), bf16[64,2,256]{2,1,0:T(2,128)(2,1)S(1)}, u32[]{:S(2)}, u32[]{:S(2)}) async-start(bf16[64,2,256]{2,1,0:T(2,128)(2,1)} %reshape.501), calls=%async_computation.3 | async-start | bytes 131072 | tf_op jit(solution)/shard_map/all_to_all | solution.py:160
  196.6 27.7 %reduce-scatter.6.cloned.1.call-start = ((), (), s32[]{:S(2)}) async-start(), calls=%async_computation.10 | async-start | bytes 327680 | tf_op jit(solution)/shard_map/reduce_scatter | solution.py:163
  196.9 1.7 copy-start.20
  206.5 17.8 %copy-start.8 = (bf16[32,512]{1,0:T(8,128)(2,1)S(1)}, bf16[32,512]{1,0:T(8,128)(2,1)}, u32[]{:S(2)}) copy-start(bf16[32,512]{1,0:T(8,128)(2,1)} %param.16) | copy-start | bytes 98308
  206.5 18.8 %copy-start.13 = (bf16[512,64]{0,1:T(8,128)(2,1)S(1)}, bf16[512,64]{0,1:T(8,128)(2,1)}, u32[]{:S(2)}) copy-start(bf16[512,64]{0,1:T(8,128)(2,1)} %param.27) | copy-start | bytes 196612
  206.5 18.8 %copy-start.15 = (f32[512]{0:T(512)S(1)}, f32[512]{0:T(512)}, u32[]{:S(2)}) copy-start(f32[512]{0:T(512)} %param.26) | copy-start | bytes 6148
  209.9 149.0 %reduce-scatter.8.cloned.1.call-start = ((), (), s32[]{:S(2)}) async-start(), calls=%async_computation.11 | async-start | bytes 1966080 | tf_op jit(solution)/shard_map/reduce_scatter | solution.py:214
  225.3 12.0 %copy-start.7 = (bf16[32,512]{1,0:T(8,128)(2,1)}, bf16[32,512]{1,0:T(8,128)(2,1)S(1)}, u32[]{:S(2)}) copy-start(bf16[32,512]{1,0:T(8,128)(2,1)S(1)} %get-tuple-element.12) | copy-start | bytes 98308
  336.5 0.9 copy-start.6
  336.5 0.9 copy-start.17
  336.5 36.1 %copy-start.10 = (bf16[32,32]{1,0:T(8,128)(2,1)S(1)}, bf16[32,32]{1,0:T(8,128)(2,1)}, u32[]{:S(2)}) copy-start(bf16[32,32]{1,0:T(8,128)(2,1)} %copy-done.9) | copy-start | bytes 6148
  336.5 36.1 %copy-start.12 = (bf16[32,32]{1,0:T(8,128)(2,1)S(1)}, bf16[32,32]{1,0:T(8,128)(2,1)}, u32[]{:S(2)}) copy-start(bf16[32,32]{1,0:T(8,128)(2,1)} %copy-done.11) | copy-start | bytes 6148
  360.9 28.9 %all-to-all-start.4 = ((bf16[64,6,512]{2,1,0:T(8,128)(2,1)}), bf16[64,6,512]{2,1,0:T(8,128)(2,1)}, u32[]{:S(2)}, u32[]{:S(2)}) async-start(bf16[64,6,512]{2,1,0:T(8,128)(2,1)} %reshape.407), calls=%async_computation.7 | async-start | bytes 1048576 | tf_op jit(solution)/shard_map/all_to_all | solution.py:220
Sparse Core Ops, SparseCore 0:
  38.9 46.1 all-reduce.6
  155.0 23.7 reduce-scatter.3
  210.1 14.2 reduce-scatter.5
  336.6 22.2 reduce-scatter.7
where the time goes:
time: 404 us; the launch traced here: 403 us
  waiting for transfers between devices  136 us (34%)
  blocking collectives  113 us (28%)
  starting transfers between devices  50.9 us (13%)
  local copies, waits for them, and re-layouts  43.6 us (11%)
  matrix products  30 us (7%)
  other arithmetic  14.6 us (4%)
  between operations  14.4 us (4%)
    all_to_all x1, blocking collectives, body(): lax.all_to_all(padded_rows[source_token].reshape(expert_count, capacity,...  70.5 us
    psum x1, waiting for transfers between devices, body(): lax.psum(jnp.dot(normed_part, w_latent, preferred_element_type=jnp.float3...  40.8 us
    reduce_scatter x1, waiting for transfers between devices, body(): lax.psum_scatter(jnp.dot(activity, expert_down[0], preferred_element_type...  21.5 us
    reduce_scatter x1, waiting for transfers between devices, body(): lax.psum_scatter(jnp.concatenate([numerator, denominator[:, :, None]], ax...  21 us
    all_to_all x1, waiting for transfers between devices, body(): got_packed = lax.all_to_all(packed[sent_row], 'tok', 0, 0, tiled=True)  15.7 us
    all_to_all x1, waiting for transfers between devices, body(): lax.all_to_all(expert_share.reshape(peer_count, capacity, quarter_width),...  15.5 us
    reduce_scatter x1, waiting for transfers between devices, body(): lax.psum_scatter(jnp.dot(head_out, w_out, preferred_element_type=jnp.floa...  14 us
    all_to_all x1, starting transfers between devices, body(): got_ints = lax.all_to_all(send_ints, 'tok', 0, 0, tiled=True)  13.1 us
  transfers between devices with their start and end apart: 8, of which 7 were waited for; matrix products, arithmetic and copies ran while one was open for 5% of the time, Pallas kernels for 0%

commit v1 on v0

--- a/solution.py
+++ b/solution.py
@@ -81,8 +81,9 @@
     normed_part = lax.dynamic_slice_in_dim(
         normed_attn, head_index * quarter_width, quarter_width, 1
     )
-    compressed = lax.psum(
-        jnp.dot(normed_part, w_latent, preferred_element_type=jnp.float32), "head"
+    compressed = jnp.sum(
+        lax.all_gather(jnp.dot(normed_part, w_latent, preferred_element_type=jnp.float32), "head"),
+        axis=0,
     )
     latent_new = compressed[:, :LATENT]
     latent_new = latent_new * lax.rsqrt(

time: 404 us -> 378 us (0.936)
  waiting for transfers between devices: 136 us -> 93.7 us
  blocking collectives: 113 us -> 123 us
    psum x1 -> x0, waiting for transfers between devices: 40.8 us -> none  [body(): lax.psum(jnp.dot(normed_part, w_latent, preferred_element_type=jnp.float3...]
    all_gather x0 -> x1, blocking collectives: none -> 9.51 us  [body(): lax.all_gather(jnp.dot(normed_part, w_latent, preferred_element_type=jnp....]
  transfers between devices with their start and end apart: 8 -> 7, of which waited for: 7 -> 6; matrix products, arithmetic and copies ran while one was open for 5% -> 7% of each run, Pallas kernels for 0% -> 0%
where the time goes in v1:
time: 378 us; the launch traced here: 376 us
  blocking collectives  123 us (33%)
  waiting for transfers between devices  93.7 us (25%)
  starting transfers between devices  53.9 us (14%)
  local copies, waits for them, and re-layouts  46.8 us (12%)
  matrix products  29.4 us (8%)
  other arithmetic  15.4 us (4%)
  between operations  14.3 us (4%)
    all_to_all x1, blocking collectives, body(): lax.all_to_all(padded_rows[source_token].reshape(expert_count, capacity,...  70.5 us
    reduce_scatter x1, waiting for transfers between devices, body(): lax.psum_scatter(jnp.concatenate([numerator, denominator[:, :, None]], ax...  21.1 us
    reduce_scatter x1, waiting for transfers between devices, body(): lax.psum_scatter(jnp.dot(activity, expert_down[0], preferred_element_type...  20.8 us
    all_to_all x1, waiting for transfers between devices, body(): lax.all_to_all(expert_share.reshape(peer_count, capacity, quarter_width),...  16.2 us
    all_to_all x1, starting transfers between devices, body(): got_packed = lax.all_to_all(packed[sent_row], 'tok', 0, 0, tiled=True)  15.6 us
    reduce_scatter x1, waiting for transfers between devices, body(): lax.psum_scatter(jnp.dot(head_out, w_out, preferred_element_type=jnp.floa...  14 us
    all_to_all x1, waiting for transfers between devices, body(): got_packed = lax.all_to_all(packed[sent_row], 'tok', 0, 0, tiled=True)  13.9 us
    all_to_all x1, starting transfers between devices, body(): got_ints = lax.all_to_all(send_ints, 'tok', 0, 0, tiled=True)  13.3 us
  transfers between devices with their start and end apart: 7, of which 6 were waited for; matrix products, arithmetic and copies ran while one was open for 7% of the time, Pallas kernels for 0%

profile of v1, /device:TPU:1, one launch (start us, length us, event | category | flops | bytes accessed | tf_op | source)
XLA Modules:
  0.0 376.2 jit_solution(5864585484302895217)
XLA Ops:
  7.2 1.3 compare_select_fusion.3
  9.1 1.4 gather_fusion
  10.6 1.4 gather_fusion.1
  12.7 13.3 %all-to-all-start = ((s32[64,1,2]{2,1,0:T(1,128)}), s32[64,1,2]{2,1,0:T(1,128)}, u32[]{:S(2)}, u32[]{:S(2)}) async-start(s32[64,1,2]{2,1,0:T(1,128)} %copy.107), calls=%async_computation | async-start | bytes 65536 | tf_op jit(solution)/shard_map/all_to_all | solution.py:122
  26.1 1.2 convert_element_type.98
  27.8 10.5 %all_gather.15 = bf16[32,2048]{1,0:T(8,128)(2,1)S(1)} all-gather(bf16[32,512]{1,0:T(8,128)(2,1)} %param.16), channel_id=1, replica_groups=mesh['tok'=64,'head'=4] {'head'}, dimensions={1}, use_global_device_ids=true | all-gather | bytes 163840 | tf_op jit(solution)/shard_map/all_gather | solution.py:77
  41.9 1.3 fusion.45
  43.2 9.5 %all-gather = f32[128,576]{1,0:T(8,128)S(1)} all-gather(f32[32,576]{1,0:T(8,128)S(1)} %fusion.45), channel_id=2, replica_groups=mesh['tok'=64,'head'=4] {'head'}, dimensions={0}, use_global_device_ids=true | all-gather | bytes 368640 | tf_op jit(solution)/shard_map/all_gather | solution.py:85
  53.0 1.3 fusion.16
  55.1 1.0 subtract_convert_fusion
  57.6 1.0 concatenate.52.clone
  58.7 1.6 gather_fusion.3
  60.3 15.6 %all-to-all-start.1 = ((bf16[64,5,576]{2,1,0:T(8,128)(2,1)}), bf16[64,5,576]{2,1,0:T(8,128)(2,1)}, u32[]{:S(2)}, u32[]{:S(2)}) async-start(bf16[64,5,576]{2,1,0:T(8,128)(2,1)} %gather_fusion.3), calls=%async_computation.1 | async-start | bytes 1310720 | tf_op jit(solution)/shard_map/all_to_all | solution.py:121
  79.0 2.5 copy.117
  82.0 13.9 %all-to-all-done.1 = bf16[64,5,576]{2,1,0:T(8,128)(2,1)} async-done(((bf16[64,5,576]{2,1,0:T(8,128)(2,1)}), bf16[64,5,576]{2,1,0:T(8,128)(2,1)}, u32[]{:S(2)}, u32[]{:S(2)}) %all-to-all-start.1) | async-done | bytes 368672 | tf_op jit(solution)/shard_map/all_to_all | solution.py:121
  95.9 1.8 gather_fusion.4
  98.5 11.4 %all_gather.18 = bf16[32,16,576]{2,0,1:T(8,128)(2,1)S(1)} all-gather(bf16[32,4,576]{2,0,1:T(8,128)(2,1)S(1)} %copy.113), channel_id=1, replica_groups=mesh['tok'=64,'head'=4] {'head'}, dimensions={1}, use_global_device_ids=true | all-gather | bytes 737280 | tf_op jit(solution)/shard_map/all_gather | solution.py:131
  110.2 6.9 %convert_reduce_fusion = (f32[512]{0:T(512)}, bf16[512,2496]{0,1:T(8,128)(2,1)}) fusion(pred[512,2496]{0,1:T(32,128)(4,1)S(1)} %copy-done.1, bf16[512,576]{1,0:T(8,128)(2,1)S(1)} %bitcast.108, bf16[2496,576]{0,1:T(8,128)(2,1)} %param.23), kind=kOutput, calls=%fused_computation.11 | convolution fusion | flops 1478589952 | bytes 7301120 | tf_op jit(solution)/shard_map/qc,pc->qp/dot_general | solution.py:37
  117.1 0.9 broadcast_in_dim.142
  118.0 4.4 %copy.115 = bf16[512,2496]{1,0:T(8,128)(2,1)} copy(bf16[512,2496]{0,1:T(8,128)(2,1)} %get-tuple-element.32) | data formatting | bytes 5111808 | tf_op jit(solution)/shard_map/exp | solution.py:44
  122.4 4.1 %fusion = f32[32,16,512]{2,1,0:T(8,128)S(1)} fusion(bf16[32,16,2496]{2,1,0:T(8,128)(2,1)} %bitcast.105, bf16[2496,576]{0,1:T(8,128)(2,1)} %param.23, pred[32,2496]{1,0:T(8,128)(4,1)S(1)} %compare_and_fusion), kind=kOutput, calls=%fused_computation.15 | convolution fusion | flops 1309900800 | bytes 6371328 | tf_op jit(solution)/shard_map/khp,pl->khl/dot_general | solution.py:45
  126.6 1.5 copy.119
  128.4 1.8 fusion.35
  131.0 21.1 %reduce-scatter.4.cloned.1.call-done = f32[32,4,513]{2,0,1:T(8,128)} async-done(((f32[32,16,513]{2,0,1:T(8,128)}), f32[32,4,513]{2,0,1:T(8,128)}) %reduce-scatter.4.cloned.1.call-update) | async-done | bytes 262672 | tf_op jit(solution)/shard_map/reduce_scatter | solution.py:135
  152.1 0.9 slice_reduce_fusion
  153.0 1.4 fusion.17
  157.0 13.1 %all-to-all-start.2 = ((bf16[64,2,256]{2,1,0:T(2,128)(2,1)}), bf16[64,2,256]{2,1,0:T(2,128)(2,1)S(1)}, u32[]{:S(2)}, u32[]{:S(2)}) async-start(bf16[64,2,256]{2,1,0:T(2,128)(2,1)} %reshape.502), calls=%async_computation.3 | async-start | bytes 131072 | tf_op jit(solution)/shard_map/all_to_all | solution.py:161
  170.4 1.6 gather_fusion.9
  172.1 7.7 %all-to-all-done.2 = bf16[64,2,256]{2,1,0:T(2,128)(2,1)S(1)} async-done(((bf16[64,2,256]{2,1,0:T(2,128)(2,1)}), bf16[64,2,256]{2,1,0:T(2,128)(2,1)S(1)}, u32[]{:S(2)}, u32[]{:S(2)}) %all-to-all-start.2) | async-done | bytes 65568 | tf_op jit(solution)/shard_map/all_to_all | solution.py:161
  180.6 2.8 fusion.62
  183.7 14.0 %reduce-scatter.6.cloned.1.call-done = f32[32,512]{1,0:T(8,128)} async-done(((f32[32,2048]{1,0:T(8,128)}), f32[32,512]{1,0:T(8,128)}) %reduce-scatter.6.cloned.1.call-update) | async-done | bytes 65552 | tf_op jit(solution)/shard_map/reduce_scatter | solution.py:164
  197.7 1.0 fusion.40
  198.9 11.8 %all-reduce.4 = (f32[32]{0:T(128)S(1)}, f32[32,64]{1,0:T(8,128)S(1)}) all-reduce(f32[32]{0:T(128)S(1)} %get-tuple-element.11, f32[32,64]{1,0:T(8,128)S(1)} %fusion.41), channel_id=1, replica_groups=mesh['tok'=64,'head'=4] {'head'}, use_global_device_ids=true, to_apply=%region_12.13 | all-reduce | flops 2080 | bytes 16640 | tf_op jit(solution)/shard_map/psum | solution.py:173
  210.7 9.1 %all_gather.19 = bf16[32,2048]{1,0:T(8,128)(2,1)S(1)} all-gather(bf16[32,512]{1,0:T(8,128)(2,1)S(1)} %fusion.39), channel_id=1, replica_groups=mesh['tok'=64,'head'=4] {'head'}, dimensions={1}, use_global_device_ids=true | all-gather | bytes 163840 | tf_op jit(solution)/shard_map/all_gather | solution.py:200
  219.9 3.1 gather_fusion.7
  223.0 3.7 reshape.405
  226.6 70.5 %all_to_all.39 = bf16[64,6,2048]{2,1,0:T(8,128)(2,1)} all-to-all(bf16[64,6,2048]{2,1,0:T(8,128)(2,1)} %reshape.405), channel_id=1, replica_groups=mesh['tok'=64,'head'=4] {'tok'}, dimensions={0} | all-to-all | bytes 3145728 | tf_op jit(solution)/shard_map/all_to_all | solution.py:204
  297.1 3.7 reshape.406
  300.8 3.6 fusion.8
  304.4 5.5 %convolution_convert_fusion = bf16[384,2048]{1,0:T(8,128)(2,1)} fusion(bf16[1,352,2048]{2,1,0:T(8,128)(2,1)} %param.31, bf16[384,2048]{1,0:T(8,128)(2,1)} %reshape.406, bf16[1,2048,352]{1,2,0:T(8,128)(2,1)} %param.30, f32[384,352]{0,1:T(8,128)} %fusion.8), kind=kOutput, calls=%fused_computation.14 | convolution fusion | flops 1108893696 | bytes 6569984 | tf_op jit(solution)/shard_map/dot_general | solution.py:216
  311.6 20.8 %reduce-scatter.8.cloned.1.call-done = bf16[384,512]{1,0:T(8,128)(2,1)} async-done(((bf16[384,2048]{1,0:T(8,128)(2,1)}), bf16[384,512]{1,0:T(8,128)(2,1)}) %reduce-scatter.8.cloned.1.call-update) | async-done | bytes 393232 | tf_op jit(solution)/shard_map/reduce_scatter | solution.py:215
  332.3 1.9 reshape.407
  334.2 11.7 %all-to-all-start.4 = ((bf16[64,6,512]{2,1,0:T(8,128)(2,1)}), bf16[64,6,512]{2,1,0:T(8,128)(2,1)}, u32[]{:S(2)}, u32[]{:S(2)}) async-start(bf16[64,6,512]{2,1,0:T(8,128)(2,1)} %reshape.407), calls=%async_computation.7 | async-start | bytes 1048576 | tf_op jit(solution)/shard_map/all_to_all | solution.py:221
  347.0 16.2 %all-to-all-done.4 = bf16[64,6,512]{2,1,0:T(8,128)(2,1)} async-done(((bf16[64,6,512]{2,1,0:T(8,128)(2,1)}), bf16[64,6,512]{2,1,0:T(8,128)(2,1)}, u32[]{:S(2)}, u32[]{:S(2)}) %all-to-all-start.4) | async-done | bytes 393248 | tf_op jit(solution)/shard_map/all_to_all | solution.py:221
  363.2 1.2 reshape.408
  364.4 1.7 gather_fusion.8
  366.0 1.8 reshape.489
  367.8 1.9 multiply_reduce_fusion
  (133 shorter events, 20.6 us)
Async XLA Ops:
  7.2 32.1 %copy-start = (bf16[2048,768]{1,0:T(8,128)(2,1)S(1)}, bf16[2048,768]{1,0:T(8,128)(2,1)}, u32[]{:S(2)}) copy-start(bf16[2048,768]{1,0:T(8,128)(2,1)} %param.18) | copy-start | bytes 9437188
  12.7 47.6 %all-to-all-start = ((s32[64,1,2]{2,1,0:T(1,128)}), s32[64,1,2]{2,1,0:T(1,128)}, u32[]{:S(2)}, u32[]{:S(2)}) async-start(s32[64,1,2]{2,1,0:T(1,128)} %copy.107), calls=%async_computation | async-start | bytes 65536 | tf_op jit(solution)/shard_map/all_to_all | solution.py:122
  52.8 4.9 %copy-start.2 = (f32[32,576]{1,0:T(8,128)}, f32[32,576]{1,0:T(8,128)S(1)}, u32[]{:S(2)}) copy-start(f32[32,576]{1,0:T(8,128)S(1)} %reduce_sum.102) | copy-start | bytes 221188
  52.8 3.4 copy-start.19
  52.9 2.2 copy-start.17
  55.1 2.6 copy-start.9
  55.1 2.5 copy-start.11
  60.3 18.2 %copy-start.14 = (s32[2496]{0:T(1024)S(1)}, s32[2496]{0:T(1024)}, u32[]{:S(2)}) copy-start(s32[2496]{0:T(1024)} %iota_add_fusion) | copy-start | bytes 29956
  60.3 35.6 %all-to-all-start.1 = ((bf16[64,5,576]{2,1,0:T(8,128)(2,1)}), bf16[64,5,576]{2,1,0:T(8,128)(2,1)}, u32[]{:S(2)}, u32[]{:S(2)}) async-start(bf16[64,5,576]{2,1,0:T(8,128)(2,1)} %gather_fusion.3), calls=%async_computation.1 | async-start | bytes 1310720 | tf_op jit(solution)/shard_map/all_to_all | solution.py:121
  75.9 76.2 %reduce-scatter.4.cloned.1.call-start = ((), (), s32[]{:S(2)}) async-start(), calls=%async_computation.8 | async-start | bytes 1638400 | tf_op jit(solution)/shard_map/reduce_scatter | solution.py:135
  97.8 19.3 %copy-start.4 = (bf16[32,5,576]{2,1,0:T(8,128)(2,1)}, bf16[32,5,576]{2,1,0:T(8,128)(2,1)S(1)}, u32[]{:S(2)}) copy-start(bf16[32,5,576]{2,1,0:T(8,128)(2,1)S(1)} %gather_fusion.4) | copy-start | bytes 552964
  97.8 12.4 %copy-start.1 = (pred[512,2496]{0,1:T(32,128)(4,1)S(1)}, pred[512,2496]{0,1:T(32,128)(4,1)}, u32[]{:S(2)}) copy-start(pred[512,2496]{0,1:T(32,128)(4,1)} %copy.117) | copy-start | bytes 3833860
  97.9 0.7 copy-start.6
  126.6 1.5 copy-start.15
  126.6 1.6 copy-start.20
  126.6 1.6 copy-start.5
  157.0 22.8 %all-to-all-start.2 = ((bf16[64,2,256]{2,1,0:T(2,128)(2,1)}), bf16[64,2,256]{2,1,0:T(2,128)(2,1)S(1)}, u32[]{:S(2)}, u32[]{:S(2)}) async-start(bf16[64,2,256]{2,1,0:T(2,128)(2,1)} %reshape.502), calls=%async_computation.3 | async-start | bytes 131072 | tf_op jit(solution)/shard_map/all_to_all | solution.py:161
  170.1 27.7 %reduce-scatter.6.cloned.1.call-start = ((), (), s32[]{:S(2)}) async-start(), calls=%async_computation.9 | async-start | bytes 327680 | tf_op jit(solution)/shard_map/reduce_scatter | solution.py:164
  170.4 1.7 copy-start.21
  179.9 17.8 %copy-start.8 = (bf16[32,512]{1,0:T(8,128)(2,1)S(1)}, bf16[32,512]{1,0:T(8,128)(2,1)}, u32[]{:S(2)}) copy-start(bf16[32,512]{1,0:T(8,128)(2,1)} %param.16) | copy-start | bytes 98308
  179.9 18.8 %copy-start.13 = (bf16[512,64]{0,1:T(8,128)(2,1)S(1)}, bf16[512,64]{0,1:T(8,128)(2,1)}, u32[]{:S(2)}) copy-start(bf16[512,64]{0,1:T(8,128)(2,1)} %param.27) | copy-start | bytes 196612
  179.9 18.8 %copy-start.16 = (f32[512]{0:T(512)S(1)}, f32[512]{0:T(512)}, u32[]{:S(2)}) copy-start(f32[512]{0:T(512)} %param.26) | copy-start | bytes 6148
  183.4 149.0 %reduce-scatter.8.cloned.1.call-start = ((), (), s32[]{:S(2)}) async-start(), calls=%async_computation.10 | async-start | bytes 1966080 | tf_op jit(solution)/shard_map/reduce_scatter | solution.py:215
  198.7 12.0 %copy-start.7 = (bf16[32,512]{1,0:T(8,128)(2,1)}, bf16[32,512]{1,0:T(8,128)(2,1)S(1)}, u32[]{:S(2)}) copy-start(bf16[32,512]{1,0:T(8,128)(2,1)S(1)} %get-tuple-element.12) | copy-start | bytes 98308
  309.9 0.9 copy-start.3
  309.9 0.9 copy-start.18
  309.9 1.0 copy-start.10
  309.9 1.0 copy-start.12
  334.2 28.9 %all-to-all-start.4 = ((bf16[64,6,512]{2,1,0:T(8,128)(2,1)}), bf16[64,6,512]{2,1,0:T(8,128)(2,1)}, u32[]{:S(2)}, u32[]{:S(2)}) async-start(bf16[64,6,512]{2,1,0:T(8,128)(2,1)} %reshape.407), calls=%async_computation.7 | async-start | bytes 1048576 | tf_op jit(solution)/shard_map/all_to_all | solution.py:221
Sparse Core Ops, SparseCore 0:
  128.3 23.7 reduce-scatter.3
  183.5 14.2 reduce-scatter.5
  310.1 22.2 reduce-scatter.7
